TPU v7x, 128 devices: a whole 4x4x4 slice. The times are simulated.
128 devices in a mesh: rep: 4 (over x), fsdp: 2 (over core), tp: 16 (over z, y).
Axes of the slice: x: 4, y: 4, z: 4, core: 2. Of those that a mesh axis runs over, the one named last changes fastest.
Arguments:
- tokens: bfloat16 [8192, 2048], P(('rep', 'fsdp'), 'tp'), may hold values from -6 to 6
- cotangent: bfloat16 [8192, 2048], P(('rep', 'fsdp'), 'tp'), may hold values from -6 to 6
- frame_mask: int32 [8192], P(('rep', 'fsdp')), may hold values 0 or 1
- ln_gain: bfloat16 [2048], P('tp'), may hold values from 0.099609375 to 1.8984375
- ln_bias: bfloat16 [2048], P('tp'), may hold values from -3 to 3
- weight_in: bfloat16 [2048, 8192], P('fsdp', 'tp'), may hold values from -0.1875 to 0.1875
- weight_out: bfloat16 [8192, 2048], P('tp', 'fsdp'), may hold values from -0.09375 to 0.09375
- blocks_in: int32 [16, 64], P('fsdp', 'tp'), may hold values 0 or 1
- blocks_out: int32 [64, 16], P('tp', 'fsdp'), may hold values 0 or 1
Outputs:
- block_out: bfloat16 [8192, 2048], P(('rep', 'fsdp'), 'tp')
- input_grad: bfloat16 [8192, 2048], P(('rep', 'fsdp'), 'tp')
- grad_in: float32 [2048, 8192], P('fsdp', 'tp')
- grad_out: float32 [8192, 2048], P('tp', 'fsdp')
- grad_gain: float32 [2048], P('tp')
- grad_bias: float32 [2048], P('tp')
All inputs are finite; a program needn't handle non-finite values. No bound on the sum of `frame_mask` or of `blocks_in` or of `blocks_out` on one device may be relied on, other than what follows from the above.
Results may differ from a plain program's by a relative error of at most 0.019.
Values may be sent and summed in bfloat16 or wider, within the bound.
No kernel may reach another device: no remote copies, remote signals or barrier semaphores. Data moves between devices by JAX's collectives and lax.ppermute only.
A program may use at most 128 MiB of HBM per device.

v0:
```python
from functools import partial
import jax
import jax.numpy as jnp
from jax import lax
from jax.sharding import PartitionSpec as P

BLK = 128


def apply_blocks(weight, blocks, kind):
    row_blocks, col_blocks = blocks.shape
    shaped = weight.reshape(row_blocks, BLK, col_blocks, BLK)
    keeper = blocks.astype(kind)[:, None, :, None]
    return (shaped * keeper).reshape(weight.shape)


def contract_rows(left, right):
    return lax.dot_general(
        left, right, (((0,), (0,)), ((), ())), preferred_element_type=jnp.float32
    )


def contract_cols(left, right):
    return lax.dot_general(
        left, right, (((1,), (1,)), ((), ())), preferred_element_type=jnp.float32
    )


def on_device(
    tokens, cotangent, frame_mask, ln_gain, ln_bias, weight_in, weight_out, blocks_in, blocks_out
):
    whole_rows, whole_grad, gain_full, bias_full = (
        lax.all_gather(tokens, "tp", axis=1, tiled=True),
        lax.all_gather(cotangent, "tp", axis=1, tiled=True),
        lax.all_gather(ln_gain, "tp", axis=0, tiled=True),
        lax.all_gather(ln_bias, "tp", axis=0, tiled=True),
    )
    masked_in = apply_blocks(weight_in, blocks_in, jnp.bfloat16)
    masked_out = apply_blocks(weight_out, blocks_out, jnp.bfloat16)
    full_in, full_out = (
        lax.all_gather(masked_in, "fsdp", axis=0, tiled=True),
        lax.all_gather(masked_out, "fsdp", axis=1, tiled=True),
    )
    width = whole_rows.shape[1]
    own_width = tokens.shape[1]
    col_start = lax.axis_index("tp") * own_width
    gelu_exact = partial(jax.nn.gelu, approximate=False)
    values = whole_rows.astype(jnp.float32)
    centre = jnp.mean(values, axis=1, keepdims=True)
    centred = values - centre
    inv_std = lax.rsqrt(jnp.mean(centred * centred, axis=1, keepdims=True) + 1e-05)
    normed = centred * inv_std
    scaled = (normed * gain_full.astype(jnp.float32) + bias_full.astype(jnp.float32)).astype(
        jnp.bfloat16
    )
    hidden = jnp.dot(scaled, full_in, preferred_element_type=jnp.float32)
    active = gelu_exact(hidden).astype(jnp.bfloat16)
    partial_out = jnp.dot(active, full_out, preferred_element_type=jnp.float32)
    branch = lax.psum_scatter(
        partial_out.astype(jnp.bfloat16), "tp", scatter_dimension=1, tiled=True
    ).astype(jnp.float32)
    block_out = (tokens.astype(jnp.float32) + branch).astype(jnp.bfloat16)
    flags = frame_mask[:, None].astype(jnp.bfloat16)
    chosen = whole_grad * flags
    chosen_own = cotangent * flags
    back_active = contract_cols(chosen, full_out)
    unused, gelu_back = jax.vjp(gelu_exact, hidden)
    back_hidden = gelu_back(back_active)[0].astype(jnp.bfloat16)
    partial_normed = contract_cols(back_hidden, full_in)
    normed_own = lax.dynamic_slice_in_dim(normed, col_start, own_width, 1)
    gain_own = ln_gain.astype(jnp.float32)
    back_normed = lax.psum_scatter(
        partial_normed.astype(jnp.bfloat16), "tp", scatter_dimension=1, tiled=True
    ).astype(jnp.float32)
    back_scaled = back_normed * gain_own
    sum_plain = jnp.sum(back_scaled, axis=1)
    sum_cross = jnp.sum(back_scaled * normed_own, axis=1)
    sum_plain, sum_cross = lax.psum((sum_plain, sum_cross), "tp")
    mean_plain = (sum_plain / width)[:, None]
    mean_cross = (sum_cross / width)[:, None]
    back_rows = inv_std * (back_scaled - mean_plain - normed_own * mean_cross)
    input_grad = (chosen_own.astype(jnp.float32) + back_rows).astype(jnp.bfloat16)
    local_gain = jnp.sum(back_normed * normed_own, axis=0)
    local_bias = jnp.sum(back_normed, axis=0)
    grad_gain, grad_bias = lax.psum((local_gain, local_bias), ("rep", "fsdp"))
    term_in = contract_rows(scaled, back_hidden)
    term_out = contract_rows(active, chosen)
    shard_in, shard_out = (
        lax.psum_scatter(
            term_in.astype(jnp.bfloat16), "fsdp", scatter_dimension=0, tiled=True
        ).astype(jnp.float32),
        lax.psum_scatter(
            term_out.astype(jnp.bfloat16), "fsdp", scatter_dimension=1, tiled=True
        ).astype(jnp.float32),
    )
    shard_in, shard_out = (
        lax.psum(shard_in.astype(jnp.bfloat16), "rep").astype(jnp.float32),
        lax.psum(shard_out.astype(jnp.bfloat16), "rep").astype(jnp.float32),
    )
    grad_in = apply_blocks(shard_in, blocks_in, jnp.float32)
    grad_out = apply_blocks(shard_out, blocks_out, jnp.float32)
    return (block_out, input_grad, grad_in, grad_out, grad_gain, grad_bias)


def solution(mesh):
    placed = (
        P(("rep", "fsdp"), "tp"),
        P(("rep", "fsdp"), "tp"),
        P(("rep", "fsdp")),
        P("tp"),
        P("tp"),
        P("fsdp", "tp"),
        P("tp", "fsdp"),
        P("fsdp", "tp"),
        P("tp", "fsdp"),
    )
    return jax.shard_map(
        on_device,
        mesh=mesh,
        in_specs=placed,
        out_specs=(
            P(("rep", "fsdp"), "tp"),
            P(("rep", "fsdp"), "tp"),
            P("fsdp", "tp"),
            P("tp", "fsdp"),
            P("tp"),
            P("tp"),
        ),
        check_vma=False,
    )
```

profile of v0, /device:TPU:0, one launch (start us, length us, event | category | flops | bytes accessed | tf_op | source)
XLA Modules:
  0.0 492.1 jit_solution(3719068611543885792)
XLA Ops:
  7.2 0.7 all-gather.7.cloned.1.call-update
  7.9 0.8 fusion.34
  8.7 0.1 copy.17
  8.8 0.3 mul.149
  9.2 2.4 bitcast_multiply_fusion.3
  11.7 0.2 mul.155
  12.0 1.2 bitcast_multiply_fusion.2
  13.2 0.5 all-gather.13.cloned.1.call-update
  13.8 22.1 %all-gather = bf16[16,1,128]{2,1,0:T(2,128)(2,1)S(1)} all-gather(bf16[1,1,128]{2,1,0:T(2,128)(2,1)S(1)} %bitcast.45), channel_id=1, replica_groups=mesh['rep'=4,'fsdp'=2,'tp'=16] {'tp'}, dimensions={0}, use_global_device_ids=true | all-gather | bytes 4352 | tf_op jit(solution)/shard_map/all_gather | solution.py:35
  36.0 19.5 %all-gather.1 = bf16[16,1,128]{2,1,0:T(2,128)(2,1)S(1)} all-gather(bf16[1,1,128]{2,1,0:T(2,128)(2,1)S(1)} %bitcast.44), channel_id=1, replica_groups=mesh['rep'=4,'fsdp'=2,'tp'=16] {'tp'}, dimensions={0}, use_global_device_ids=true | all-gather | bytes 4352 | tf_op jit(solution)/shard_map/all_gather | solution.py:36
  55.5 14.8 %all-gather.7.cloned.1.call-done = bf16[1024,2048]{1,0:T(8,128)(2,1)} async-done(((bf16[1024,128]{1,0:T(8,128)(2,1)}), bf16[1024,2048]{1,0:T(8,128)(2,1)}) %all-gather.7.cloned.1.call-update) | async-done | bytes 4194320 | tf_op jit(solution)/shard_map/all_gather | solution.py:33
  70.4 3.0 convert_reduce_fusion
  73.4 0.5 copy-done
  73.8 1.2 fusion.2
  75.1 10.1 %all-gather.9.cloned.1.call-done = bf16[2048,512]{1,0:T(8,128)(2,1)} async-done(((bf16[1024,512]{1,0:T(8,128)(2,1)}), bf16[2048,512]{1,0:T(8,128)(2,1)}) %all-gather.9.cloned.1.call-update) | async-done | bytes 2097168 | tf_op jit(solution)/shard_map/all_gather | solution.py:41
  85.1 10.5 %multiply_convert_fusion = (bf16[1024,512]{1,0:T(8,128)(2,1)S(1)}, f32[1024,512]{1,0:T(8,128)}, f32[1024,512]{1,0:T(8,128)}) fusion(bf16[2048,512]{1,0:T(8,128)(2,1)} %all-gather.9.cloned.1.call-done, f32[2048]{0:T(1024)S(1)} %bitcast.42, f32[2048]{0:T(1024)S(1)} %bitcast.40, f32[1024]{0:T(1024)S(1)} %add_rsqrt_fusion, ...), kind=kOutput, calls=%fused_computation.21 | convolution fusion | flops 2194145280 | bytes 11558912 | tf_op jit(solution)/shard_map/dot_general | solution.py:56
  95.6 5.8 %all-gather.11.cloned.1.call-done = bf16[512,2048]{1,0:T(8,128)(2,1)} async-done(((bf16[512,1024]{1,0:T(8,128)(2,1)}), bf16[512,2048]{1,0:T(8,128)(2,1)}) %all-gather.11.cloned.1.call-update) | async-done | bytes 2097168 | tf_op jit(solution)/shard_map/all_gather | solution.py:42
  101.4 61.1 %all-gather.13.cloned.1.call-done = bf16[1024,2048]{1,0:T(8,128)(2,1)} async-done(((bf16[1024,128]{1,0:T(8,128)(2,1)}), bf16[1024,2048]{1,0:T(8,128)(2,1)}) %all-gather.13.cloned.1.call-update) | async-done | bytes 4194320 | tf_op jit(solution)/shard_map/all_gather | solution.py:34
  162.5 7.1 %add_convert_fusion.1 = bf16[1024,512]{1,0:T(8,128)(2,1)S(1)} fusion(f32[1024,512]{1,0:T(8,128)} %get-tuple-element.17, f32[1024,512]{1,0:T(8,128)} %get-tuple-element.22, bf16[512,2048]{1,0:T(8,128)(2,1)} %all-gather.11.cloned.1.call-done, bf16[1024,2048]{1,0:T(8,128)(2,1)} %all-gather.13.cloned.1.call-done, bf16[1024]{0:T(1024)(128)(2,1)S(1)} %convert_element_type.88), kind=kOutput, calls=%fused_computation.18 | convolution fusion | flops 2156920832 | bytes 11536384 | tf_op jit(solution)/shard_map/dot_general | solution.py:24
  169.7 1.0 copy-done.14
  170.7 4.4 convolution_convert_fusion.2
  175.1 0.2 reduce-scatter.11.cloned.1.call-start
  175.4 6.0 %fusion.7 = bf16[512,2048]{1,0:T(8,128)(2,1)} fusion(bf16[1024,512]{1,0:T(8,128)(2,1)S(1)} %get-tuple-element.16, bf16[1024,2048]{1,0:T(8,128)(2,1)} %all-gather.13.cloned.1.call-done, bf16[1024]{0:T(1024)(128)(2,1)S(1)} %convert_element_type.88), kind=kOutput, calls=%fused_computation.14 | convolution fusion | flops 2150629376 | bytes 7342080 | tf_op jit(solution)/shard_map/dot_general | solution.py:18
  181.4 5.3 %reduce-scatter.9.cloned.1.call-done = bf16[1024,512]{1,0:T(8,128)(2,1)} async-done(((bf16[2048,512]{1,0:T(8,128)(2,1)}), bf16[1024,512]{1,0:T(8,128)(2,1)}) %reduce-scatter.9.cloned.1.call-update) | async-done | bytes 1048592 | tf_op jit(solution)/shard_map/reduce_scatter | solution.py:89
  186.7 16.6 %reduce-scatter.11.cloned.1.call-done = bf16[512,1024]{1,0:T(8,128)(2,1)} async-done(((bf16[512,2048]{1,0:T(8,128)(2,1)}), bf16[512,1024]{1,0:T(8,128)(2,1)}) %reduce-scatter.11.cloned.1.call-update) | async-done | bytes 1048592 | tf_op jit(solution)/shard_map/reduce_scatter | solution.py:92
  203.4 5.5 %convolution_convert_fusion = bf16[1024,2048]{1,0:T(8,128)(2,1)} fusion(bf16[1024,512]{1,0:T(8,128)(2,1)} %copy-done.14, bf16[2048,512]{1,0:T(8,128)(2,1)S(1)} %copy-done.11), kind=kOutput, calls=%fused_computation.6 | convolution fusion | flops 2149580800 | bytes 7340032 | tf_op jit(solution)/shard_map/dot_general | solution.py:24
  208.9 6.4 %copy.21 = bf16[1024,2048]{0,1:T(8,128)(2,1)} copy(bf16[1024,2048]{1,0:T(8,128)(2,1)} %convolution_convert_fusion) | data formatting | bytes 8388608
  215.4 1.6 copy-done.12
  217.0 5.5 %convolution_convert_fusion.1 = bf16[1024,2048]{1,0:T(8,128)(2,1)} fusion(bf16[1024,512]{1,0:T(8,128)(2,1)} %copy-done.13, bf16[512,2048]{1,0:T(8,128)(2,1)S(1)} %copy-done.12), kind=kOutput, calls=%fused_computation.7 | convolution fusion | flops 2149580800 | bytes 7340032 | tf_op jit(solution)/shard_map/dot_general | solution.py:58
  222.5 6.4 %copy.19 = bf16[1024,2048]{0,1:T(8,128)(2,1)} copy(bf16[1024,2048]{1,0:T(8,128)(2,1)} %convolution_convert_fusion.1) | data formatting | bytes 8388608
  228.9 0.1 copy.18
  229.0 6.4 %fusion = f32[1024,2048]{1,0:T(8,128)} fusion(bf16[1024,2048]{1,0:T(8,128)(2,1)} %all-gather.7.cloned.1.call-done, f32[1024]{0:T(1024)S(1)} %add_rsqrt_fusion, f32[1024]{0:T(1024)S(1)} %broadcast_multiply_fusion.2), kind=kLoop, calls=%fused_computation.2 | loop fusion | flops 6291456 | bytes 12591104 | tf_op jit(solution)/shard_map/mul | solution.py:52
  235.4 30.6 %all-reduce.5.cloned.1.call-done = (bf16[1024,512]{1,0:T(8,128)(2,1)}, bf16[512,1024]{1,0:T(8,128)(2,1)}) async-done(((bf16[1024,512]{1,0:T(8,128)(2,1)}, bf16[512,1024]{1,0:T(8,128)(2,1)}), (bf16[1024,512]{1,0:T(8,128)(2,1)}, bf16[512,1024]{1,0:T(8,128)(2,1)})) %all-reduce.5.cloned.1.call-update) | async-done | bytes 2097168 | tf_op jit(solution)/shard_map/psum | solution.py:97
  266.0 0.3 mul.177
  266.4 0.9 copy-done.4
  267.3 1.7 bitcast_multiply_fusion.1
  268.9 0.2 mul.180
  269.1 1.0 copy-done.3
  270.2 2.0 bitcast_multiply_fusion
  272.2 75.3 %reduce-scatter.15.cloned.1.call-done = bf16[128,1024]{1,0:T(8,128)(2,1)} async-done(((bf16[2048,1024]{1,0:T(8,128)(2,1)}), bf16[128,1024]{1,0:T(8,128)(2,1)}) %reduce-scatter.15.cloned.1.call-update) | async-done | bytes 262160
  347.4 1.1 copy.22
  348.5 79.2 %reduce-scatter.13.cloned.1.call-done = bf16[128,1024]{1,0:T(8,128)(2,1)} async-done(((bf16[2048,1024]{1,0:T(8,128)(2,1)}), bf16[128,1024]{1,0:T(8,128)(2,1)}) %reduce-scatter.13.cloned.1.call-update) | async-done | bytes 262160
  427.7 1.1 copy.20
  428.8 0.8 add_convert_fusion.4
  429.6 1.4 fusion.29
  431.0 13.5 %all-reduce.1 = (f32[128]{0:T(128)}, f32[128]{0:T(128)}) all-reduce(f32[128]{0:T(128)S(1)} %get-tuple-element.6, f32[128]{0:T(128)S(1)} %get-tuple-element.9), channel_id=1, replica_groups=mesh['rep'=4,'fsdp'=2,'tp'=16] {'rep','fsdp'}, use_global_device_ids=true, to_apply=%region_13.0 | all-reduce | flops 256 | bytes 2048 | tf_op jit(solution)/shard_map/psum | solution.py:85
  444.5 38.7 %all-reduce = (f32[1024]{0:T(1024)S(1)}, f32[1024]{0:T(1024)S(1)}) all-reduce(f32[1024]{0:T(1024)S(1)} %get-tuple-element.7, f32[1024]{0:T(1024)S(1)} %get-tuple-element.8), channel_id=1, replica_groups=mesh['rep'=4,'fsdp'=2,'tp'=16] {'tp'}, use_global_device_ids=true, to_apply=%region_7.0 | all-reduce | flops 2048 | bytes 16384 | tf_op jit(solution)/shard_map/psum | solution.py:78
  483.2 2.4 fusion.27
  (48 shorter events, 0.5 us)
Async XLA Ops:
  7.2 63.2 %all-gather.7.cloned.1.call-start = ((), (), s32[]{:S(2)}) async-start(), calls=%async_computation.4 | async-start | bytes 4456448 | tf_op jit(solution)/shard_map/all_gather | solution.py:33
  7.9 77.2 %all-gather.9.cloned.1.call-start = ((), (), s32[]{:S(2)}) async-start(), calls=%async_computation.5 | async-start | bytes 3145728 | tf_op jit(solution)/shard_map/all_gather | solution.py:41
  9.2 2.5 copy-start.8
  9.2 2.7 copy-start.2
  11.6 89.8 %all-gather.11.cloned.1.call-start = ((), (), s32[]{:S(2)}) async-start(), calls=%async_computation.6 | async-start | bytes 3145728 | tf_op jit(solution)/shard_map/all_gather | solution.py:42
  11.9 1.9 copy-start.10
  11.9 24.1 %copy-start.9 = (bf16[128]{0:T(256)(128)(2,1)S(1)}, bf16[128]{0:T(256)(128)(2,1)}, u32[]{:S(2)}) copy-start(bf16[128]{0:T(256)(128)(2,1)} %param.13) | copy-start | bytes 772
  11.9 43.6 %copy-start.7 = (s32[1024]{0:T(1024)S(1)}, s32[1024]{0:T(1024)}, u32[]{:S(2)}) copy-start(s32[1024]{0:T(1024)} %param.11) | copy-start | bytes 12292
  13.2 149.3 %all-gather.13.cloned.1.call-start = ((), (), s32[]{:S(2)}) async-start(), calls=%async_computation.7 | async-start | bytes 4456448 | tf_op jit(solution)/shard_map/all_gather | solution.py:34
  13.8 173.0 %reduce-scatter.9.cloned.1.call-start = ((), (), s32[]{:S(2)}) async-start(), calls=%async_computation.8 | async-start | bytes 3145728 | tf_op jit(solution)/shard_map/reduce_scatter | solution.py:89
  70.4 3.4 copy-start
  95.6 79.8 %copy-start.13 = (bf16[1024,512]{1,0:T(8,128)(2,1)}, bf16[1024,512]{1,0:T(8,128)(2,1)S(1)}, u32[]{:S(2)}) copy-start(bf16[1024,512]{1,0:T(8,128)(2,1)S(1)} %get-tuple-element.16) | copy-start | bytes 3145732
  162.5 8.1 %copy-start.1 = (bf16[1024,2048]{1,0:T(8,128)(2,1)S(1)}, bf16[1024,2048]{1,0:T(8,128)(2,1)}, u32[]{:S(2)}) copy-start(bf16[1024,2048]{1,0:T(8,128)(2,1)} %all-gather.7.cloned.1.call-done) | copy-start | bytes 12582916
  169.6 1.0 copy-start.14
  175.1 28.2 %reduce-scatter.11.cloned.1.call-start = ((), (), s32[]{:S(2)}) async-start(), calls=%async_computation.9 | async-start | bytes 3145728 | tf_op jit(solution)/shard_map/reduce_scatter | solution.py:92
  181.3 22.1 %copy-start.11 = (bf16[2048,512]{1,0:T(8,128)(2,1)S(1)}, bf16[2048,512]{1,0:T(8,128)(2,1)}, u32[]{:S(2)}) copy-start(bf16[2048,512]{1,0:T(8,128)(2,1)} %all-gather.9.cloned.1.call-done) | copy-start | bytes 6291460
  181.4 84.7 %all-reduce.5.cloned.1.call-start = ((), (), s32[]{:S(2)}) async-start(), calls=%async_computation.12 | async-start | bytes 4194304 | tf_op jit(solution)/shard_map/psum | solution.py:97
  203.3 144.1 %reduce-scatter.15.cloned.1.call-start = ((), (), s32[]{:S(2)}) async-start(), calls=%async_computation.11 | async-start | bytes 4456448
  215.3 1.6 copy-start.12
  215.3 212.4 %reduce-scatter.13.cloned.1.call-start = ((), (), s32[]{:S(2)}) async-start(), calls=%async_computation.10 | async-start | bytes 4456448
  266.0 1.2 copy-start.4
  268.9 1.2 copy-start.3
  270.2 158.7 %copy-start.5 = (bf16[1024,128]{1,0:T(8,128)(2,1)S(1)}, bf16[1024,128]{1,0:T(8,128)(2,1)}, u32[]{:S(2)}) copy-start(bf16[1024,128]{1,0:T(8,128)(2,1)} %param.9) | copy-start | bytes 786436
  272.2 211.0 %copy-start.6 = (bf16[1024,128]{1,0:T(8,128)(2,1)S(1)}, bf16[1024,128]{1,0:T(8,128)(2,1)}, u32[]{:S(2)}) copy-start(bf16[1024,128]{1,0:T(8,128)(2,1)} %param.10) | copy-start | bytes 786436
Sparse Core Ops, SparseCore 0:
  10.1 60.2 all-gather.6
  72.6 12.4 all-gather.8
  86.8 14.6 all-gather.10
  103.4 59.0 all-gather.12
  175.2 11.4 reduce-scatter.8
  189.6 13.6 reduce-scatter.10
  205.8 60.2 all-reduce.4
  269.7 77.6 reduce-scatter.14
  350.8 76.9 reduce-scatter.12
where the time goes:
time: 493 us; the launch traced here: 492 us
  waiting for transfers between devices  300 us (61%)
  blocking collectives  93.8 us (19%)
  matrix products  39 us (8%)
  other arithmetic  23.2 us (5%)
  local copies, waits for them, and re-layouts  21.3 us (4%)
  between operations  14.1 us (3%)
    unnamed x11, waiting for transfers between devices  156 us
    all_gather x1, waiting for transfers between devices, on_device(): lax.all_gather(cotangent, 'tp', axis=1, tiled=True)  61.1 us
    psum x1, blocking collectives, on_device(): sum_plain, sum_cross = lax.psum((sum_plain, sum_cross), 'tp')  38.7 us
    psum x1, waiting for transfers between devices, on_device(): lax.psum(shard_in.astype(jnp.bfloat16), 'rep').astype(jnp.float32)  30.6 us
    all_gather x1, blocking collectives, on_device(): lax.all_gather(ln_gain, 'tp', axis=0, tiled=True)  22.1 us
    unnamed x34, local copies, waits for them, and re-layouts  20 us
    all_gather x1, blocking collectives, on_device(): lax.all_gather(ln_bias, 'tp', axis=0, tiled=True)  19.5 us
    reduce_scatter x1, waiting for transfers between devices, on_device(): lax.psum_scatter(term_out.astype(jnp.bfloat16), 'fsdp', scatter_dimension...  16.6 us
  transfers between devices with their start and end apart: 9, of which 9 were waited for; matrix products, arithmetic and copies ran while one was open for 12% of the time, Pallas kernels for 0%

commit v1 on v0

--- a/solution.py
+++ b/solution.py
@@ -94,7 +94,7 @@
         ).astype(jnp.float32),
     )
     shard_in, shard_out = (
-        lax.psum(shard_in.astype(jnp.bfloat16), "rep").astype(jnp.float32),
+        jnp.sum(lax.all_gather(shard_in.astype(jnp.bfloat16), "rep"), axis=0).astype(jnp.float32),
         lax.psum(shard_out.astype(jnp.bfloat16), "rep").astype(jnp.float32),
     )
     grad_in = apply_blocks(shard_in, blocks_in, jnp.float32)

time: 493 us -> 476 us (0.966)
  waiting for transfers between devices: 300 us -> 280 us
    reduce_scatter x1, waiting for transfers between devices: 16.6 us -> 3.73 us  [on_device(): lax.psum_scatter(term_out.astype(jnp.bfloat16), 'fsdp', scatter_dimension...]
    all_gather x1, waiting for transfers between devices: 61.1 us -> 50.8 us  [on_device(): lax.all_gather(cotangent, 'tp', axis=1, tiled=True)]
    reduce_scatter x1, waiting for transfers between devices: 5.31 us -> 0.02 us  [on_device(): lax.psum_scatter(term_in.astype(jnp.bfloat16), 'fsdp', scatter_dimension=...]
    unnamed x11 -> x12, waiting for transfers between devices: 156 us -> 160 us
  transfers between devices with their start and end apart: 9 -> 10, of which waited for: 9 -> 8; matrix products, arithmetic and copies ran while one was open for 12% -> 16% of each run, Pallas kernels for 0% -> 0%
where the time goes in v1:
time: 476 us; the launch traced here: 475 us
  waiting for transfers between devices  280 us (59%)
  blocking collectives  93.7 us (20%)
  matrix products  38.6 us (8%)
  other arithmetic  26.8 us (6%)
  local copies, waits for them, and re-layouts  20.9 us (4%)
  between operations  14.4 us (3%)
    unnamed x12, waiting for transfers between devices  160 us
    all_gather x1, waiting for transfers between devices, on_device(): lax.all_gather(cotangent, 'tp', axis=1, tiled=True)  50.8 us
    psum x1, blocking collectives, on_device(): sum_plain, sum_cross = lax.psum((sum_plain, sum_cross), 'tp')  38.7 us
    psum x1, waiting for transfers between devices, on_device(): lax.psum(shard_out.astype(jnp.bfloat16), 'rep').astype(jnp.float32)  32.8 us
    all_gather x1, blocking collectives, on_device(): lax.all_gather(ln_gain, 'tp', axis=0, tiled=True)  22.1 us
    unnamed x34, local copies, waits for them, and re-layouts  19.6 us
    all_gather x1, blocking collectives, on_device(): lax.all_gather(ln_bias, 'tp', axis=0, tiled=True)  19.5 us
    all_gather x1, waiting for transfers between devices, on_device(): lax.all_gather(tokens, 'tp', axis=1, tiled=True)  14.8 us
  transfers between devices with their start and end apart: 10, of which 8 were waited for; matrix products, arithmetic and copies ran while one was open for 16% of the time, Pallas kernels for 0%

profile of v1, /device:TPU:0, one launch (start us, length us, event | category | flops | bytes accessed | tf_op | source)
XLA Modules:
  0.0 475.3 jit_solution(168967057289806560)
XLA Ops:
  7.2 0.7 all-gather.9.cloned.1.call-update
  7.9 0.8 fusion.34
  8.7 0.1 copy.17
  8.8 0.3 mul.149
  9.2 2.4 bitcast_multiply_fusion.3
  11.7 0.7 all-gather.15.cloned.1.call-update
  12.4 0.2 mul.155
  12.7 1.1 bitcast_multiply_fusion.2
  13.9 22.1 %all-gather.1 = bf16[16,1,128]{2,1,0:T(2,128)(2,1)S(1)} all-gather(bf16[1,1,128]{2,1,0:T(2,128)(2,1)S(1)} %bitcast.47), channel_id=1, replica_groups=mesh['rep'=4,'fsdp'=2,'tp'=16] {'tp'}, dimensions={0}, use_global_device_ids=true | all-gather | bytes 4352 | tf_op jit(solution)/shard_map/all_gather | solution.py:35
  36.1 19.5 %all-gather.2 = bf16[16,1,128]{2,1,0:T(2,128)(2,1)S(1)} all-gather(bf16[1,1,128]{2,1,0:T(2,128)(2,1)S(1)} %bitcast.46), channel_id=1, replica_groups=mesh['rep'=4,'fsdp'=2,'tp'=16] {'tp'}, dimensions={0}, use_global_device_ids=true | all-gather | bytes 4352 | tf_op jit(solution)/shard_map/all_gather | solution.py:36
  55.6 14.8 %all-gather.9.cloned.1.call-done = bf16[1024,2048]{1,0:T(8,128)(2,1)} async-done(((bf16[1024,128]{1,0:T(8,128)(2,1)}), bf16[1024,2048]{1,0:T(8,128)(2,1)}) %all-gather.9.cloned.1.call-update) | async-done | bytes 4194320 | tf_op jit(solution)/shard_map/all_gather | solution.py:33
  70.4 3.0 convert_reduce_fusion
  73.4 0.5 copy-done
  73.8 1.2 fusion.2
  75.1 10.1 %all-gather.11.cloned.1.call-done = bf16[2048,512]{1,0:T(8,128)(2,1)} async-done(((bf16[1024,512]{1,0:T(8,128)(2,1)}), bf16[2048,512]{1,0:T(8,128)(2,1)}) %all-gather.11.cloned.1.call-update) | async-done | bytes 2097168 | tf_op jit(solution)/shard_map/all_gather | solution.py:41
  85.1 10.5 %multiply_convert_fusion = (bf16[1024,512]{1,0:T(8,128)(2,1)S(1)}, f32[1024,512]{1,0:T(8,128)}, f32[1024,512]{1,0:T(8,128)}) fusion(bf16[2048,512]{1,0:T(8,128)(2,1)} %all-gather.11.cloned.1.call-done, f32[2048]{0:T(1024)S(1)} %bitcast.44, f32[2048]{0:T(1024)S(1)} %bitcast.42, f32[1024]{0:T(1024)S(1)} %add_rsqrt_fusion, ...), kind=kOutput, calls=%fused_computation.21 | convolution fusion | flops 2194145280 | bytes 11558912 | tf_op jit(solution)/shard_map/dot_general | solution.py:56
  95.6 50.8 %all-gather.15.cloned.1.call-done = bf16[1024,2048]{1,0:T(8,128)(2,1)} async-done(((bf16[1024,128]{1,0:T(8,128)(2,1)}), bf16[1024,2048]{1,0:T(8,128)(2,1)}) %all-gather.15.cloned.1.call-update) | async-done | bytes 4194320 | tf_op jit(solution)/shard_map/all_gather | solution.py:34
  146.4 6.0 %fusion.7 = bf16[512,2048]{1,0:T(8,128)(2,1)} fusion(bf16[1024,512]{1,0:T(8,128)(2,1)S(1)} %get-tuple-element.14, bf16[1024,2048]{1,0:T(8,128)(2,1)} %all-gather.15.cloned.1.call-done, bf16[1024]{0:T(1024)(128)(2,1)S(1)} %convert_element_type.92), kind=kOutput, calls=%fused_computation.14 | convolution fusion | flops 2150629376 | bytes 7342080 | tf_op jit(solution)/shard_map/dot_general | solution.py:18
  152.4 0.2 reduce-scatter.9.cloned.1.call-start
  152.6 7.8 %all-gather.13.cloned.1.call-done = bf16[512,2048]{1,0:T(8,128)(2,1)} async-done(((bf16[512,1024]{1,0:T(8,128)(2,1)}), bf16[512,2048]{1,0:T(8,128)(2,1)}) %all-gather.13.cloned.1.call-update) | async-done | bytes 2097168 | tf_op jit(solution)/shard_map/all_gather | solution.py:42
  160.4 6.6 %add_convert_fusion.1 = bf16[1024,512]{1,0:T(8,128)(2,1)S(1)} fusion(f32[1024,512]{1,0:T(8,128)S(1)} %copy-done.14, f32[1024,512]{1,0:T(8,128)} %get-tuple-element.20, bf16[512,2048]{1,0:T(8,128)(2,1)} %all-gather.13.cloned.1.call-done, bf16[1024,2048]{1,0:T(8,128)(2,1)} %all-gather.15.cloned.1.call-done, bf16[1024]{0:T(1024)(128)(2,1)S(1)} %convert_element_type.92), kind=kOutput, calls=%fused_computation.18 | convolution fusion | flops 2156920832 | bytes 11536384 | tf_op jit(solution)/shard_map/dot_general | solution.py:24
  167.0 1.0 copy-done.13
  168.0 4.4 convolution_convert_fusion.2
  172.5 3.7 reduce-scatter.11.cloned.1.call-done
  176.3 5.5 %convolution_convert_fusion = bf16[1024,2048]{1,0:T(8,128)(2,1)} fusion(bf16[1024,512]{1,0:T(8,128)(2,1)} %copy-done.13, bf16[2048,512]{1,0:T(8,128)(2,1)S(1)} %copy-done.10), kind=kOutput, calls=%fused_computation.6 | convolution fusion | flops 2149580800 | bytes 7340032 | tf_op jit(solution)/shard_map/dot_general | solution.py:24
  181.8 6.4 %copy.21 = bf16[1024,2048]{0,1:T(8,128)(2,1)} copy(bf16[1024,2048]{1,0:T(8,128)(2,1)} %convolution_convert_fusion) | data formatting | bytes 8388608
  188.3 2.1 copy-done.11
  190.4 5.6 %convolution_convert_fusion.1 = bf16[1024,2048]{1,0:T(8,128)(2,1)} fusion(bf16[1024,512]{1,0:T(8,128)(2,1)} %copy-done.12, bf16[512,2048]{1,0:T(8,128)(2,1)S(1)} %copy-done.11), kind=kOutput, calls=%fused_computation.7 | convolution fusion | flops 2149580800 | bytes 7340032 | tf_op jit(solution)/shard_map/dot_general | solution.py:58
  195.9 6.4 %copy.19 = bf16[1024,2048]{0,1:T(8,128)(2,1)} copy(bf16[1024,2048]{1,0:T(8,128)(2,1)} %convolution_convert_fusion.1) | data formatting | bytes 8388608
  202.4 0.3 all-gather.17.cloned.1.call-start
  202.7 0.3 all-gather.17.cloned.1.call-update
  203.1 6.5 %fusion = f32[1024,2048]{1,0:T(8,128)} fusion(bf16[1024,2048]{1,0:T(8,128)(2,1)} %all-gather.9.cloned.1.call-done, f32[1024]{0:T(1024)S(1)} %add_rsqrt_fusion, f32[1024]{0:T(1024)S(1)} %broadcast_multiply_fusion.2), kind=kLoop, calls=%fused_computation.2 | loop fusion | flops 6291456 | bytes 12591104 | tf_op jit(solution)/shard_map/mul | solution.py:52
  209.6 32.8 %all-reduce.4.cloned.1.call-done = bf16[512,1024]{1,0:T(8,128)(2,1)} async-done(((bf16[512,1024]{1,0:T(8,128)(2,1)}), bf16[512,1024]{1,0:T(8,128)(2,1)}) %all-reduce.4.cloned.1.call-update) | async-done | bytes 1048592 | tf_op jit(solution)/shard_map/psum | solution.py:98
  242.4 0.2 mul.180
  242.6 1.0 copy-done.3
  243.6 2.0 bitcast_multiply_fusion
  245.6 79.2 %reduce-scatter.15.cloned.1.call-done = bf16[128,1024]{1,0:T(8,128)(2,1)} async-done(((bf16[2048,1024]{1,0:T(8,128)(2,1)}), bf16[128,1024]{1,0:T(8,128)(2,1)}) %reduce-scatter.15.cloned.1.call-update) | async-done | bytes 262160
  324.8 1.1 copy.22
  326.0 79.3 %reduce-scatter.13.cloned.1.call-done = bf16[128,1024]{1,0:T(8,128)(2,1)} async-done(((bf16[2048,1024]{1,0:T(8,128)(2,1)}), bf16[128,1024]{1,0:T(8,128)(2,1)}) %reduce-scatter.13.cloned.1.call-update) | async-done | bytes 262160
  405.2 1.1 copy.20
  406.4 1.4 fusion.29
  407.8 13.4 %all-reduce.1 = (f32[128]{0:T(128)}, f32[128]{0:T(128)}) all-reduce(f32[128]{0:T(128)S(1)} %get-tuple-element.6, f32[128]{0:T(128)S(1)} %get-tuple-element.9), channel_id=1, replica_groups=mesh['rep'=4,'fsdp'=2,'tp'=16] {'rep','fsdp'}, use_global_device_ids=true, to_apply=%region_13.0 | all-reduce | flops 256 | bytes 2048 | tf_op jit(solution)/shard_map/psum | solution.py:85
  421.1 38.7 %all-reduce = (f32[1024]{0:T(1024)S(1)}, f32[1024]{0:T(1024)S(1)}) all-reduce(f32[1024]{0:T(1024)S(1)} %get-tuple-element.7, f32[1024]{0:T(1024)S(1)} %get-tuple-element.8), channel_id=1, replica_groups=mesh['rep'=4,'fsdp'=2,'tp'=16] {'tp'}, use_global_device_ids=true, to_apply=%region_7.0 | all-reduce | flops 2048 | bytes 16384 | tf_op jit(solution)/shard_map/psum | solution.py:78
  459.8 0.8 add_convert_fusion.4
  460.6 2.4 fusion.27
  463.0 3.5 reduce_sum.70
  466.5 0.3 mul.177
  466.8 1.7 bitcast_multiply_fusion.1
  (52 shorter events, 0.6 us)
Async XLA Ops:
  7.2 63.2 %all-gather.9.cloned.1.call-start = ((), (), s32[]{:S(2)}) async-start(), calls=%async_computation.4 | async-start | bytes 4456448 | tf_op jit(solution)/shard_map/all_gather | solution.py:33
  7.9 77.2 %all-gather.11.cloned.1.call-start = ((), (), s32[]{:S(2)}) async-start(), calls=%async_computation.5 | async-start | bytes 3145728 | tf_op jit(solution)/shard_map/all_gather | solution.py:41
  9.2 3.3 copy-start.7
  9.2 3.5 copy-start.2
  11.6 134.7 %all-gather.15.cloned.1.call-start = ((), (), s32[]{:S(2)}) async-start(), calls=%async_computation.7 | async-start | bytes 4456448 | tf_op jit(solution)/shard_map/all_gather | solution.py:34
  12.4 148.0 %all-gather.13.cloned.1.call-start = ((), (), s32[]{:S(2)}) async-start(), calls=%async_computation.6 | async-start | bytes 3145728 | tf_op jit(solution)/shard_map/all_gather | solution.py:42
  12.7 1.3 copy-start.9
  12.7 23.4 %copy-start.8 = (bf16[128]{0:T(256)(128)(2,1)S(1)}, bf16[128]{0:T(256)(128)(2,1)}, u32[]{:S(2)}) copy-start(bf16[128]{0:T(256)(128)(2,1)} %param.13) | copy-start | bytes 772
  12.7 42.9 %copy-start.6 = (s32[1024]{0:T(1024)S(1)}, s32[1024]{0:T(1024)}, u32[]{:S(2)}) copy-start(s32[1024]{0:T(1024)} %param.11) | copy-start | bytes 12292
  13.9 162.4 %reduce-scatter.11.cloned.1.call-start = ((), (), s32[]{:S(2)}) async-start(), calls=%async_computation.9 | async-start | bytes 3145728 | tf_op jit(solution)/shard_map/reduce_scatter | solution.py:92
  70.4 3.4 copy-start
  95.6 56.8 %copy-start.12 = (bf16[1024,512]{1,0:T(8,128)(2,1)}, bf16[1024,512]{1,0:T(8,128)(2,1)S(1)}, u32[]{:S(2)}) copy-start(bf16[1024,512]{1,0:T(8,128)(2,1)S(1)} %get-tuple-element.14) | copy-start | bytes 3145732
  152.3 8.0 %copy-start.14 = (f32[1024,512]{1,0:T(8,128)S(1)}, f32[1024,512]{1,0:T(8,128)}, u32[]{:S(2)}) copy-start(f32[1024,512]{1,0:T(8,128)} %get-tuple-element.15) | copy-start | bytes 6291460
  152.4 50.3 %reduce-scatter.9.cloned.1.call-start = ((), (), s32[]{:S(2)}) async-start(), calls=%async_computation.8 | async-start | bytes 3145728 | tf_op jit(solution)/shard_map/reduce_scatter | solution.py:89
  160.4 7.6 %copy-start.1 = (bf16[1024,2048]{1,0:T(8,128)(2,1)S(1)}, bf16[1024,2048]{1,0:T(8,128)(2,1)}, u32[]{:S(2)}) copy-start(bf16[1024,2048]{1,0:T(8,128)(2,1)} %all-gather.9.cloned.1.call-done) | copy-start | bytes 12582916
  167.0 1.0 copy-start.13
  172.4 3.9 copy-start.10
  172.4 70.0 %all-reduce.4.cloned.1.call-start = ((), (), s32[]{:S(2)}) async-start(), calls=%async_computation.10 | async-start | bytes 2097152 | tf_op jit(solution)/shard_map/psum | solution.py:98
  176.2 148.6 %reduce-scatter.15.cloned.1.call-start = ((), (), s32[]{:S(2)}) async-start(), calls=%async_computation.13 | async-start | bytes 4456448
  188.2 2.1 copy-start.11
  188.3 217.0 %reduce-scatter.13.cloned.1.call-start = ((), (), s32[]{:S(2)}) async-start(), calls=%async_computation.12 | async-start | bytes 4456448
  202.4 260.6 %all-gather.17.cloned.1.call-start = ((), (), s32[]{:S(2)}) async-start(), calls=%async_computation.11 | async-start | bytes 5242880 | tf_op jit(solution)/shard_map/all_gather | solution.py:97
  242.4 1.2 copy-start.3
  243.6 216.2 %copy-start.4 = (bf16[1024,128]{1,0:T(8,128)(2,1)S(1)}, bf16[1024,128]{1,0:T(8,128)(2,1)}, u32[]{:S(2)}) copy-start(bf16[1024,128]{1,0:T(8,128)(2,1)} %param.9) | copy-start | bytes 786436
  245.6 215.0 %copy-start.5 = (bf16[1024,128]{1,0:T(8,128)(2,1)S(1)}, bf16[1024,128]{1,0:T(8,128)(2,1)}, u32[]{:S(2)}) copy-start(bf16[1024,128]{1,0:T(8,128)(2,1)} %param.10) | copy-start | bytes 786436
Sparse Core Ops, SparseCore 0:
  10.1 60.2 all-gather.8
  72.6 12.4 all-gather.10
  87.2 59.0 all-gather.14
  147.9 12.4 all-gather.12
  162.6 13.5 reduce-scatter.10
  179.1 13.6 reduce-scatter.8
  195.2 47.2 all-reduce.3
  246.1 78.6 reduce-scatter.14
  328.2 77.0 reduce-scatter.12
  406.9 47.4 all-gather.16
